TPU v7x, 128 devices: a whole 4x4x4 slice. The times are simulated.
128 devices in a mesh: tok: 16 (over y, z), own: 8 (over x, core).
Axes of the slice: x: 4, y: 4, z: 4, core: 2. Of those that a mesh axis runs over, the one named last changes fastest.
Arguments:
- tokens: bfloat16 [16384, 1152], P(('tok', 'own')), may hold values from -6 to 6
- norm_gain: bfloat16 [1152], replicated, may hold values from 0.099609375 to 1.8984375
- w_query: bfloat16 [1152, 1152], replicated, as said below
- w_key: bfloat16 [1152, 384], replicated, as said below
- w_value: bfloat16 [1152, 384], replicated, may hold values from -0.1875 to 0.1875
- w_output: bfloat16 [1152, 1152], replicated, may hold values from -0.1875 to 0.1875
- qkv_in: bfloat16 [64, 48, 1152], P('own', None, 'tok'), may hold values from -0.1875 to 0.1875
- q_out: bfloat16 [64, 16, 1152], P('own', None, 'tok'), may hold values from -1.5 to 1.5
- kv_out: bfloat16 [64, 32, 384], P('own', None, 'tok'), may hold values from -1.5 to 1.5
- o_in: bfloat16 [64, 16, 1152], P('own', None, 'tok'), may hold values from -0.1875 to 0.1875
- o_out: bfloat16 [64, 16, 1152], P('own', None, 'tok'), may hold values from -1.5 to 1.5
- lengths: int32 [64], replicated, may hold values from 32 to 1536, as said below
- prompt_adapter: int32 [64], replicated, may hold values from 0 to 63
- adapter_slot: int32 [64], replicated, may hold values from 0 to 63, each once
Outputs:
- mixed: bfloat16 [16384, 1152], P(('tok', 'own'))
- kv_cache: bfloat16 [16384, 768], P(('tok', 'own'))
Inputs may be any that keep to these rules, and one draw needn't show every extreme that they name: `w_query`: entries lie within 6 / sqrt(1152) of zero. `w_key`: entries lie within 6 / sqrt(1152) of zero. `lengths`: lengths sum to 16384; exactly 8 prompts are 1536 long; the others hold 32 to 128 tokens, and one of them exactly 32. `adapter_slot`: each slot appears once; slot s is row s of the adapter tables, held by own index s // 8.
All inputs are finite; a program needn't handle non-finite values.
Results may differ from a plain program's by a relative error of at most 0.02.
Values may be sent and summed in bfloat16 or wider, within the bound.
No kernel may reach another device: no remote copies, remote signals or barrier semaphores. Data moves between devices by JAX's collectives and lax.ppermute only.
A program may use at most 128 MiB of HBM per device.

v0:
```python
import math

import jax
import jax.numpy as jnp
from jax import lax
from jax.sharding import PartitionSpec as P

D = 1152
HEADS = 18
KV_HEADS = 6
HEAD_WIDTH = 64
RANK = 16
REACH = 12
KVW = 384
SEG_DEV = 5


EPS = 1e-05
THETA = 10000.0


def from_behind(block, axis, distance):
    devices = range(lax.axis_size(axis))
    route = [(i - distance, i) for i in devices if i - distance in devices]
    return lax.ppermute(block, axis, route)


def rms_norm(row_block, gain_vec):
    widened = row_block.astype(jnp.float32)
    inverse_rms = lax.rsqrt(jnp.mean(widened * widened, axis=-1, keepdims=True) + EPS)
    return (widened * inverse_rms * gain_vec.astype(jnp.float32)).astype(jnp.bfloat16)


def prompt_index(positions, lengths):
    prompt_ends = jnp.cumsum(lengths)
    prompt_starts = prompt_ends - lengths
    inside = (positions[:, None] >= prompt_starts[None, :]).astype(jnp.int32)
    segment = jnp.sum(inside, axis=1) - 1
    members = jnp.arange(lengths.shape[0], dtype=jnp.int32)[None, :] == segment[:, None]
    offset = positions - jnp.sum(jnp.where(members, prompt_starts[None, :], 0), axis=1)
    return (segment, offset, members)


def slot_lookup(adapter, adapter_slot):
    matches = jnp.arange(adapter_slot.shape[0], dtype=jnp.int32)[None, :] == adapter[:, None]
    return jnp.sum(jnp.where(matches, adapter_slot[None, :], 0), axis=1)


def rotate(vectors, offset):
    half_dim = vectors.shape[-1] // 2
    frequency = jnp.exp(
        jnp.arange(half_dim, dtype=jnp.float32) * (-2.0 * math.log(THETA) / vectors.shape[-1])
    )
    angles = offset.astype(jnp.float32)[:, None] * frequency[None, :]
    cosine = jnp.cos(angles)[:, None, :]
    sine_table = jnp.sin(angles)[:, None, :]
    first_half = vectors[..., :half_dim]
    second_half = vectors[..., half_dim:]
    return jnp.concatenate(
        [
            first_half * cosine - second_half * sine_table,
            second_half * cosine + first_half * sine_table,
        ],
        axis=-1,
    )


def adapter_terms(row_block, code_rows, a_in, pieces):
    table_count, rank_cols, in_width = a_in.shape
    projected = lax.dot_general(
        row_block,
        a_in.reshape(table_count * rank_cols, in_width),
        (((1,), (1,)), ((), ())),
        preferred_element_type=jnp.float32,
    )
    chosen = (jnp.arange(table_count, dtype=jnp.int32)[None, :] == code_rows[:, None]).astype(
        jnp.float32
    )
    low_rank = (projected.reshape(-1, table_count, rank_cols) * chosen[:, :, None]).astype(
        jnp.bfloat16
    )
    results = []
    for col_start, b_table in pieces:
        width_rank = b_table.shape[1]
        section = low_rank[:, :, col_start : col_start + width_rank].reshape(
            -1, table_count * width_rank
        )
        results.append(
            jnp.dot(
                section,
                b_table.reshape(table_count * width_rank, b_table.shape[2]),
                preferred_element_type=jnp.float32,
            ).astype(jnp.bfloat16)
        )
    return tuple(results)


def on_device(
    tokens,
    norm_gain,
    w_query,
    w_key,
    w_value,
    w_output,
    qkv_in,
    q_out,
    kv_out,
    o_in,
    o_out,
    lengths,
    prompt_adapter,
    adapter_slot,
):
    tok_rows = tokens.shape[0]
    tok_count = lax.axis_size("tok")
    own_count = lax.axis_size("own")
    per_owner = qkv_in.shape[0]
    device_here = lax.axis_index(("tok", "own"))
    positions = device_here * tok_rows + jnp.arange(tok_rows, dtype=jnp.int32)
    segment, offset, members = prompt_index(positions, lengths)
    prompt_count = lengths.shape[0]
    first_segment = segment[0]
    segment_ids = jnp.minimum(
        first_segment + jnp.arange(SEG_DEV, dtype=jnp.int32), prompt_count - 1
    )
    segment_hit = jnp.arange(prompt_count, dtype=jnp.int32)[None, :] == segment_ids[:, None]
    needed_adapter = jnp.sum(jnp.where(segment_hit, prompt_adapter[None, :], 0), axis=1)
    needed_slot = slot_lookup(needed_adapter, adapter_slot)
    code_rows = segment - first_segment
    normed = rms_norm(tokens, norm_gain)
    table_shapes = tuple((table.shape[1:] for table in (qkv_in, q_out, kv_out, o_in, o_out)))
    flat_qkv_in = qkv_in.reshape(per_owner, -1)
    flat_q_out = q_out.reshape(per_owner, -1)
    flat_kv_out = kv_out.reshape(per_owner, -1)
    flat_o_in = o_in.reshape(per_owner, -1)
    flat_o_out = o_out.reshape(per_owner, -1)
    selected = []
    gathered = (
        lax.all_gather(flat_qkv_in, ("tok", "own"), axis=0, tiled=True),
        lax.all_gather(flat_q_out, ("tok", "own"), axis=0, tiled=True),
        lax.all_gather(flat_kv_out, ("tok", "own"), axis=0, tiled=True),
        lax.all_gather(flat_o_in, ("tok", "own"), axis=0, tiled=True),
        lax.all_gather(flat_o_out, ("tok", "own"), axis=0, tiled=True),
    )
    for flat_all, table_shape in zip(gathered, table_shapes):
        shaped = flat_all.reshape(tok_count, own_count * per_owner, table_shape[0], table_shape[1])
        chosen = jnp.take(shaped, needed_slot, axis=1)
        selected.append(
            jnp.transpose(chosen, (1, 2, 0, 3)).reshape(
                SEG_DEV, table_shape[0], tok_count * table_shape[1]
            )
        )
    input_maps, query_maps, keyvalue_maps, output_in_maps, output_out_maps = selected
    delta_q, delta_k, delta_v = adapter_terms(
        normed,
        code_rows,
        input_maps,
        ((0, query_maps), (RANK, keyvalue_maps[:, :RANK]), (2 * RANK, keyvalue_maps[:, RANK:])),
    )
    base_q = jnp.dot(normed, w_query, preferred_element_type=jnp.float32)
    base_k = jnp.dot(normed, w_key, preferred_element_type=jnp.float32)
    base_v = jnp.dot(normed, w_value, preferred_element_type=jnp.float32)
    query_lin = (base_q + delta_q.astype(jnp.float32)).reshape(tok_rows, HEADS, HEAD_WIDTH)
    queries = rotate(query_lin, offset).reshape(tok_rows, D).astype(jnp.bfloat16)
    key_lin = (base_k + delta_k.astype(jnp.float32)).reshape(tok_rows, KV_HEADS, HEAD_WIDTH)
    key_rows = rotate(key_lin, offset).reshape(tok_rows, KVW).astype(jnp.bfloat16)
    value_rows = (base_v + delta_v.astype(jnp.float32)).astype(jnp.bfloat16)
    key_value = jnp.concatenate([key_rows, value_rows], axis=1)
    key_store = jnp.zeros(((REACH + 1) * tok_rows, 2 * KVW), jnp.bfloat16)
    key_store = lax.dynamic_update_slice_in_dim(key_store, key_value, REACH * tok_rows, 0)

    def advance(turn_index, loop_carry):
        moving, stored = loop_carry
        moving = from_behind(moving, ("tok", "own"), 1)
        stored = lax.dynamic_update_slice_in_dim(
            stored, moving, (REACH - 1 - turn_index) * tok_rows, 0
        )
        return (moving, stored)

    window = lax.fori_loop(0, REACH, advance, (key_value, key_store))[1]
    key_positions = (
        device_here * tok_rows
        - REACH * tok_rows
        + jnp.arange((REACH + 1) * tok_rows, dtype=jnp.int32)
    )
    key_segment = prompt_index(key_positions, lengths)[0]
    allowed = (segment[:, None] == key_segment[None, :]) & (
        key_positions[None, :] <= positions[:, None]
    )
    groups = HEADS // KV_HEADS
    key_count = window.shape[0]
    query_head_rows = queries.reshape(tok_rows, KV_HEADS, groups, HEAD_WIDTH)
    key_head_rows = window[:, :KVW].reshape(key_count, KV_HEADS, HEAD_WIDTH)
    value_head_rows = window[:, KVW:].reshape(key_count, KV_HEADS, HEAD_WIDTH)
    score_matrix = jnp.einsum(
        "qkzr,ckr->kzqc", query_head_rows, key_head_rows, preferred_element_type=jnp.float32
    ) * HEAD_WIDTH ** (-0.5)
    score_matrix = jnp.where(allowed[None, None], score_matrix, -1e30)
    top_score = jnp.max(score_matrix, axis=-1, keepdims=True)
    exp_scores = jnp.exp(score_matrix - top_score)
    row_total = jnp.sum(exp_scores, axis=-1)
    rounded_values = exp_scores.astype(jnp.bfloat16)
    summed_rows = jnp.einsum(
        "iyxv,vip->xiyp", rounded_values, value_head_rows, preferred_element_type=jnp.float32
    )
    attn_rows = (
        (summed_rows / jnp.transpose(row_total, (2, 0, 1))[..., None])
        .reshape(tok_rows, D)
        .astype(jnp.bfloat16)
    )
    delta_o = adapter_terms(attn_rows, code_rows, output_in_maps, ((0, output_out_maps),))[0]
    projected_out = jnp.dot(
        attn_rows, w_output, preferred_element_type=jnp.float32
    ) + delta_o.astype(jnp.float32)
    mixed_rows = (tokens.astype(jnp.float32) + projected_out).astype(jnp.bfloat16)
    return (mixed_rows, key_value)


def solution(mesh):
    return jax.shard_map(
        on_device,
        mesh=mesh,
        in_specs=(
            P(("tok", "own"), None),
            P(),
            P(),
            P(),
            P(),
            P(),
            P("own", None, "tok"),
            P("own", None, "tok"),
            P("own", None, "tok"),
            P("own", None, "tok"),
            P("own", None, "tok"),
            P(),
            P(),
            P(),
        ),
        out_specs=(P(("tok", "own"), None), P(("tok", "own"), None)),
        check_vma=False,
    )
```

profile of v0, /device:TPU:8, one launch (start us, length us, event | category | flops | bytes accessed | tf_op | source)
XLA Modules:
  0.0 594.2 jit_solution(6210738623967796516)
XLA Ops:
  22.9 53.1 %all-gather.8.cloned.1.call-done = bf16[1024,768]{1,0:T(8,128)(2,1)} async-done(((bf16[8,768]{1,0:T(8,128)(2,1)}), bf16[1024,768]{1,0:T(8,128)(2,1)}) %all-gather.8.cloned.1.call-update) | async-done | bytes 1572880 | tf_op jit(solution)/shard_map/all_gather | solution.py:141
  78.5 5.2 reshape.303
  83.8 8.8 %copy.54 = bf16[16,64,32,24]{2,3,1,0:T(8,128)(2,1)} copy(bf16[16,64,32,24]{1,0,3,2:T(8,128)(2,1)} %reshape.303) | data formatting | bytes 3145728 | tf_op jit(solution)/shard_map/reshape | solution.py:146
  92.5 3.4 gather_fusion.1
  96.9 45.4 %all-gather.14.cloned.1.call-done = bf16[1024,1152]{1,0:T(8,128)(2,1)} async-done(((bf16[8,1152]{1,0:T(8,128)(2,1)}), bf16[1024,1152]{1,0:T(8,128)(2,1)}) %all-gather.14.cloned.1.call-update) | async-done | bytes 2359312 | tf_op jit(solution)/shard_map/all_gather | solution.py:143
  142.3 9.6 %reshape.316 = bf16[16,64,16,72]{3,2,1,0:T(8,128)(2,1)} reshape(bf16[1024,1152]{1,0:T(8,128)(2,1)} %all-gather.14.cloned.1.call-done) | data formatting | bytes 4718592 | tf_op jit(solution)/shard_map/reshape | solution.py:146
  154.8 53.3 %all-gather.12.cloned.1.call-done = bf16[1024,1152]{1,0:T(8,128)(2,1)} async-done(((bf16[8,1152]{1,0:T(8,128)(2,1)}), bf16[1024,1152]{1,0:T(8,128)(2,1)}) %all-gather.12.cloned.1.call-update) | async-done | bytes 2359312 | tf_op jit(solution)/shard_map/all_gather | solution.py:142
  208.0 9.6 %reshape.313 = bf16[16,64,16,72]{3,2,1,0:T(8,128)(2,1)} reshape(bf16[1024,1152]{1,0:T(8,128)(2,1)} %all-gather.12.cloned.1.call-done) | data formatting | bytes 4718592 | tf_op jit(solution)/shard_map/reshape | solution.py:146
  217.6 3.6 gather_fusion.3
  221.2 52.4 %all-gather.10.cloned.1.call-done = bf16[1024,1152]{1,0:T(8,128)(2,1)} async-done(((bf16[8,1152]{1,0:T(8,128)(2,1)}), bf16[1024,1152]{1,0:T(8,128)(2,1)}) %all-gather.10.cloned.1.call-update) | async-done | bytes 2359312 | tf_op jit(solution)/shard_map/all_gather | solution.py:140
  273.6 9.6 %reshape.310 = bf16[16,64,16,72]{3,2,1,0:T(8,128)(2,1)} reshape(bf16[1024,1152]{1,0:T(8,128)(2,1)} %all-gather.10.cloned.1.call-done) | data formatting | bytes 4718592 | tf_op jit(solution)/shard_map/reshape | solution.py:146
  283.3 3.6 gather_fusion.2
  294.1 48.8 %all-gather.6.cloned.1.call-done = bf16[1024,3456]{1,0:T(8,128)(2,1)} async-done(((bf16[8,3456]{1,0:T(8,128)(2,1)}), bf16[1024,3456]{1,0:T(8,128)(2,1)}) %all-gather.6.cloned.1.call-update) | async-done | bytes 7077904 | tf_op jit(solution)/shard_map/all_gather | solution.py:139
  343.0 25.5 %reshape.301 = bf16[16,64,48,72]{3,2,1,0:T(8,128)(2,1)} reshape(bf16[1024,3456]{1,0:T(8,128)(2,1)} %all-gather.6.cloned.1.call-done) | data formatting | bytes 14155776 | tf_op jit(solution)/shard_map/reshape | solution.py:146
  368.5 6.3 %gather_fusion = bf16[5,16,48,72]{3,2,1,0:T(8,128)(2,1)} fusion(bf16[16,64,48,72]{3,2,1,0:T(8,128)(2,1)} %reshape.301, s32[1024]{0:T(1024)S(1)} %pad_clamp_fusion.1), kind=kCustom, calls=%fused_computation.3 | custom fusion | bytes 1105940 | tf_op jit(solution)/shard_map/jit(_take)/gather | solution.py:147
  391.8 153.3 %while.15 = (s32[]{:T(128)}, bf16[128,768]{1,0:T(8,128)(2,1)}, bf16[1664,768]{1,0:T(8,128)(2,1)}, s32[]{:T(128)}, s32[]{:T(128)}, /*index=5*/s32[]{:T(128)}, s32[]{:T(128)}, s32[]{:T(128)}) while((s32[]{:T(128)}, bf16[128,768]{1,0:T(8,128)(2,1)}, bf16[1664,768]{1,0:T(8,128)(2,1)}, s32[]{:T(128)}, s32[]{:T(128)}, /*index=5*/s32[]{:T(128)}, ...), condition=%wide.region_7.8_spmd, body=%wide.region_6.7_spmd.sunk | while | flops 7 | bytes 1573059 | solution.py:180
  394.0 9.3 %collective-permute-done = bf16[128,768]{1,0:T(8,128)(2,1)S(1)} collective-permute-done((bf16[128,768]{1,0:T(8,128)(2,1)}, bf16[128,768]{1,0:T(8,128)(2,1)S(1)}, u32[]{:S(2)}, u32[]{:S(2)}) %collective-permute-start) | collective-permute-done | bytes 196640 | tf_op jit(solution)/shard_map/while/body/eval_jaxpr/ppermute | solution.py:25
  406.6 9.5 %collective-permute-done = bf16[128,768]{1,0:T(8,128)(2,1)S(1)} collective-permute-done((bf16[128,768]{1,0:T(8,128)(2,1)}, bf16[128,768]{1,0:T(8,128)(2,1)S(1)}, u32[]{:S(2)}, u32[]{:S(2)}) %collective-permute-start) | collective-permute-done | bytes 196640 | tf_op jit(solution)/shard_map/while/body/eval_jaxpr/ppermute | solution.py:25
  419.3 9.5 %collective-permute-done = bf16[128,768]{1,0:T(8,128)(2,1)S(1)} collective-permute-done((bf16[128,768]{1,0:T(8,128)(2,1)}, bf16[128,768]{1,0:T(8,128)(2,1)S(1)}, u32[]{:S(2)}, u32[]{:S(2)}) %collective-permute-start) | collective-permute-done | bytes 196640 | tf_op jit(solution)/shard_map/while/body/eval_jaxpr/ppermute | solution.py:25
  432.1 9.5 %collective-permute-done = bf16[128,768]{1,0:T(8,128)(2,1)S(1)} collective-permute-done((bf16[128,768]{1,0:T(8,128)(2,1)}, bf16[128,768]{1,0:T(8,128)(2,1)S(1)}, u32[]{:S(2)}, u32[]{:S(2)}) %collective-permute-start) | collective-permute-done | bytes 196640 | tf_op jit(solution)/shard_map/while/body/eval_jaxpr/ppermute | solution.py:25
  444.9 9.5 %collective-permute-done = bf16[128,768]{1,0:T(8,128)(2,1)S(1)} collective-permute-done((bf16[128,768]{1,0:T(8,128)(2,1)}, bf16[128,768]{1,0:T(8,128)(2,1)S(1)}, u32[]{:S(2)}, u32[]{:S(2)}) %collective-permute-start) | collective-permute-done | bytes 196640 | tf_op jit(solution)/shard_map/while/body/eval_jaxpr/ppermute | solution.py:25
  457.7 9.5 %collective-permute-done = bf16[128,768]{1,0:T(8,128)(2,1)S(1)} collective-permute-done((bf16[128,768]{1,0:T(8,128)(2,1)}, bf16[128,768]{1,0:T(8,128)(2,1)S(1)}, u32[]{:S(2)}, u32[]{:S(2)}) %collective-permute-start) | collective-permute-done | bytes 196640 | tf_op jit(solution)/shard_map/while/body/eval_jaxpr/ppermute | solution.py:25
  470.5 9.5 %collective-permute-done = bf16[128,768]{1,0:T(8,128)(2,1)S(1)} collective-permute-done((bf16[128,768]{1,0:T(8,128)(2,1)}, bf16[128,768]{1,0:T(8,128)(2,1)S(1)}, u32[]{:S(2)}, u32[]{:S(2)}) %collective-permute-start) | collective-permute-done | bytes 196640 | tf_op jit(solution)/shard_map/while/body/eval_jaxpr/ppermute | solution.py:25
  483.2 9.5 %collective-permute-done = bf16[128,768]{1,0:T(8,128)(2,1)S(1)} collective-permute-done((bf16[128,768]{1,0:T(8,128)(2,1)}, bf16[128,768]{1,0:T(8,128)(2,1)S(1)}, u32[]{:S(2)}, u32[]{:S(2)}) %collective-permute-start) | collective-permute-done | bytes 196640 | tf_op jit(solution)/shard_map/while/body/eval_jaxpr/ppermute | solution.py:25
  496.0 9.5 %collective-permute-done = bf16[128,768]{1,0:T(8,128)(2,1)S(1)} collective-permute-done((bf16[128,768]{1,0:T(8,128)(2,1)}, bf16[128,768]{1,0:T(8,128)(2,1)S(1)}, u32[]{:S(2)}, u32[]{:S(2)}) %collective-permute-start) | collective-permute-done | bytes 196640 | tf_op jit(solution)/shard_map/while/body/eval_jaxpr/ppermute | solution.py:25
  508.7 9.5 %collective-permute-done = bf16[128,768]{1,0:T(8,128)(2,1)S(1)} collective-permute-done((bf16[128,768]{1,0:T(8,128)(2,1)}, bf16[128,768]{1,0:T(8,128)(2,1)S(1)}, u32[]{:S(2)}, u32[]{:S(2)}) %collective-permute-start) | collective-permute-done | bytes 196640 | tf_op jit(solution)/shard_map/while/body/eval_jaxpr/ppermute | solution.py:25
  521.5 9.5 %collective-permute-done = bf16[128,768]{1,0:T(8,128)(2,1)S(1)} collective-permute-done((bf16[128,768]{1,0:T(8,128)(2,1)}, bf16[128,768]{1,0:T(8,128)(2,1)S(1)}, u32[]{:S(2)}, u32[]{:S(2)}) %collective-permute-start) | collective-permute-done | bytes 196640 | tf_op jit(solution)/shard_map/while/body/eval_jaxpr/ppermute | solution.py:25
  534.3 9.5 %collective-permute-done = bf16[128,768]{1,0:T(8,128)(2,1)S(1)} collective-permute-done((bf16[128,768]{1,0:T(8,128)(2,1)}, bf16[128,768]{1,0:T(8,128)(2,1)S(1)}, u32[]{:S(2)}, u32[]{:S(2)}) %collective-permute-start) | collective-permute-done | bytes 196640 | tf_op jit(solution)/shard_map/while/body/eval_jaxpr/ppermute | solution.py:25
  545.2 3.4 fusion.42
  559.0 9.0 %fusion.2 = (f32[6,3,128]{2,1,0:T(4,128)S(1)}, f32[6,1664,128,3]{2,1,3,0:T(8,128)}) fusion(pred[128,1664]{0,1:T(8,128)(4,1)S(1)} %compare_and_fusion, bf16[1664,6,64,1]{0,2,3,1:T(8,128)(2,1)} %bitcast.105, bf16[128,6,3,64]{0,3,2,1:T(8,128)(2,1)S(1)} %bitcast.109), kind=kOutput, calls=%fused_computation.10 | convolution fusion | flops 502232832 | bytes 17130496 | tf_op jit(solution)/shard_map/qkzr,ckr->kzqc/dot_general | solution.py:195
  568.0 8.6 %fusion = f32[6,3,128]{2,1,0:T(4,128)S(1)} fusion(f32[6,1664,128,3]{2,1,3,0:T(8,128)} %get-tuple-element.86, f32[6,3,128]{2,1,0:T(4,128)S(1)} %get-tuple-element.85, pred[128,1664]{0,1:T(8,128)(4,1)S(1)} %compare_and_fusion), kind=kLoop, calls=%fused_computation.8 | loop fusion | flops 15333120 | bytes 15566848 | tf_op jit(solution)/shard_map/reduce_sum | solution.py:201
  576.6 9.2 %fusion.23 = bf16[128,6,3,64]{0,3,2,1:T(8,128)(2,1)S(1)} fusion(bf16[1664,6,64,1]{0,2,3,1:T(8,128)(2,1)S(1)} %bitcast.110, f32[6,1664,128,3]{2,1,3,0:T(8,128)} %get-tuple-element.86, f32[6,3,128]{2,1,0:T(4,128)S(1)} %get-tuple-element.85, pred[128,1664]{0,1:T(8,128)(4,1)S(1)} %compare_and_fusion, f32[128,6,3]{0,2,1:T(4,128)S(1)} %bitcast.117), kind=kOutput, calls=%fused_computation.36 | convolution fusion | flops 506363904 | bytes 17139712 | tf_op jit(solution)/shard_map/iyxv,vip->xiyp/dot_general | solution.py:203
  (151 shorter events, 97.7 us)
Async XLA Ops:
  7.2 547.0 %copy-start = (bf16[1152,1152]{1,0:T(8,128)(2,1)S(1)}, bf16[1152,1152]{1,0:T(8,128)(2,1)}, u32[]{:S(2)}) copy-start(bf16[1152,1152]{1,0:T(8,128)(2,1)} %param.20) | copy-start | bytes 7962628
  7.2 68.8 %all-gather.8.cloned.1.call-start = ((), (), s32[]{:S(2)}) async-start(), calls=%async_computation.1 | async-start | bytes 1585152 | tf_op jit(solution)/shard_map/all_gather | solution.py:141
  9.0 133.3 %all-gather.14.cloned.1.call-start = ((), (), s32[]{:S(2)}) async-start(), calls=%async_computation.4 | async-start | bytes 2377728 | tf_op jit(solution)/shard_map/all_gather | solution.py:143
  10.6 197.5 %all-gather.12.cloned.1.call-start = ((), (), s32[]{:S(2)}) async-start(), calls=%async_computation.3 | async-start | bytes 2377728 | tf_op jit(solution)/shard_map/all_gather | solution.py:142
  12.1 261.5 %all-gather.10.cloned.1.call-start = ((), (), s32[]{:S(2)}) async-start(), calls=%async_computation.2 | async-start | bytes 2377728 | tf_op jit(solution)/shard_map/all_gather | solution.py:140
  13.7 329.3 %all-gather.6.cloned.1.call-start = ((), (), s32[]{:S(2)}) async-start(), calls=%async_computation | async-start | bytes 7133184 | tf_op jit(solution)/shard_map/all_gather | solution.py:139
  17.7 362.5 %copy-start.10 = (f32[1152]{0:T(1024)}, f32[1152]{0:T(1024)S(1)}, u32[]{:S(2)}) copy-start(f32[1152]{0:T(1024)S(1)} %convert_element_type.88) | copy-start | bytes 13828
  21.0 359.2 %copy-start.13 = (f32[128]{0:T(128)}, f32[128]{0:T(128)S(1)}, u32[]{:S(2)}) copy-start(f32[128]{0:T(128)S(1)} %add_rsqrt_fusion) | copy-start | bytes 1540
  21.1 359.2 %copy-start.15 = (f32[128,5]{0,1:T(8,128)}, f32[128,5]{0,1:T(8,128)S(1)}, u32[]{:S(2)}) copy-start(f32[128,5]{0,1:T(8,128)S(1)} %fusion.34) | copy-start | bytes 7684
  368.5 11.8 %copy-start.1 = (bf16[128,1152]{1,0:T(8,128)(2,1)S(1)}, bf16[128,1152]{1,0:T(8,128)(2,1)}, u32[]{:S(2)}) copy-start(bf16[128,1152]{1,0:T(8,128)(2,1)} %param.18) | copy-start | bytes 884740
  389.5 159.1 %copy-start.3 = (bf16[128,768]{1,0:T(8,128)(2,1)}, bf16[128,768]{1,0:T(8,128)(2,1)S(1)}, u32[]{:S(2)}) copy-start(bf16[128,768]{1,0:T(8,128)(2,1)S(1)} %pad_maximum_fusion.1) | copy-start | bytes 589828
  391.8 11.4 %collective-permute-start = (bf16[128,768]{1,0:T(8,128)(2,1)}, bf16[128,768]{1,0:T(8,128)(2,1)S(1)}, u32[]{:S(2)}, u32[]{:S(2)}) collective-permute-start(bf16[128,768]{1,0:T(8,128)(2,1)} %get-tuple-element.115), channel_id=1, source_target_pairs={{0,1},{1,2},{2,3},{3,4},{4,5},{5,6},{6,7},{7,8},{8,9},{9,10},{10,1... | collective-permute-start | bytes 589832 | tf_op jit(solution)/shard_map/while/body/eval_jaxpr/ppermute | solution.py:25
  404.6 11.4 %collective-permute-start = (bf16[128,768]{1,0:T(8,128)(2,1)}, bf16[128,768]{1,0:T(8,128)(2,1)S(1)}, u32[]{:S(2)}, u32[]{:S(2)}) collective-permute-start(bf16[128,768]{1,0:T(8,128)(2,1)} %get-tuple-element.115), channel_id=1, source_target_pairs={{0,1},{1,2},{2,3},{3,4},{4,5},{5,6},{6,7},{7,8},{8,9},{9,10},{10,1... | collective-permute-start | bytes 589832 | tf_op jit(solution)/shard_map/while/body/eval_jaxpr/ppermute | solution.py:25
  417.4 11.4 %collective-permute-start = (bf16[128,768]{1,0:T(8,128)(2,1)}, bf16[128,768]{1,0:T(8,128)(2,1)S(1)}, u32[]{:S(2)}, u32[]{:S(2)}) collective-permute-start(bf16[128,768]{1,0:T(8,128)(2,1)} %get-tuple-element.115), channel_id=1, source_target_pairs={{0,1},{1,2},{2,3},{3,4},{4,5},{5,6},{6,7},{7,8},{8,9},{9,10},{10,1... | collective-permute-start | bytes 589832 | tf_op jit(solution)/shard_map/while/body/eval_jaxpr/ppermute | solution.py:25
  430.2 11.4 %collective-permute-start = (bf16[128,768]{1,0:T(8,128)(2,1)}, bf16[128,768]{1,0:T(8,128)(2,1)S(1)}, u32[]{:S(2)}, u32[]{:S(2)}) collective-permute-start(bf16[128,768]{1,0:T(8,128)(2,1)} %get-tuple-element.115), channel_id=1, source_target_pairs={{0,1},{1,2},{2,3},{3,4},{4,5},{5,6},{6,7},{7,8},{8,9},{9,10},{10,1... | collective-permute-start | bytes 589832 | tf_op jit(solution)/shard_map/while/body/eval_jaxpr/ppermute | solution.py:25
  443.0 11.4 %collective-permute-start = (bf16[128,768]{1,0:T(8,128)(2,1)}, bf16[128,768]{1,0:T(8,128)(2,1)S(1)}, u32[]{:S(2)}, u32[]{:S(2)}) collective-permute-start(bf16[128,768]{1,0:T(8,128)(2,1)} %get-tuple-element.115), channel_id=1, source_target_pairs={{0,1},{1,2},{2,3},{3,4},{4,5},{5,6},{6,7},{7,8},{8,9},{9,10},{10,1... | collective-permute-start | bytes 589832 | tf_op jit(solution)/shard_map/while/body/eval_jaxpr/ppermute | solution.py:25
  455.7 11.4 %collective-permute-start = (bf16[128,768]{1,0:T(8,128)(2,1)}, bf16[128,768]{1,0:T(8,128)(2,1)S(1)}, u32[]{:S(2)}, u32[]{:S(2)}) collective-permute-start(bf16[128,768]{1,0:T(8,128)(2,1)} %get-tuple-element.115), channel_id=1, source_target_pairs={{0,1},{1,2},{2,3},{3,4},{4,5},{5,6},{6,7},{7,8},{8,9},{9,10},{10,1... | collective-permute-start | bytes 589832 | tf_op jit(solution)/shard_map/while/body/eval_jaxpr/ppermute | solution.py:25
  468.5 11.4 %collective-permute-start = (bf16[128,768]{1,0:T(8,128)(2,1)}, bf16[128,768]{1,0:T(8,128)(2,1)S(1)}, u32[]{:S(2)}, u32[]{:S(2)}) collective-permute-start(bf16[128,768]{1,0:T(8,128)(2,1)} %get-tuple-element.115), channel_id=1, source_target_pairs={{0,1},{1,2},{2,3},{3,4},{4,5},{5,6},{6,7},{7,8},{8,9},{9,10},{10,1... | collective-permute-start | bytes 589832 | tf_op jit(solution)/shard_map/while/body/eval_jaxpr/ppermute | solution.py:25
  481.3 11.4 %collective-permute-start = (bf16[128,768]{1,0:T(8,128)(2,1)}, bf16[128,768]{1,0:T(8,128)(2,1)S(1)}, u32[]{:S(2)}, u32[]{:S(2)}) collective-permute-start(bf16[128,768]{1,0:T(8,128)(2,1)} %get-tuple-element.115), channel_id=1, source_target_pairs={{0,1},{1,2},{2,3},{3,4},{4,5},{5,6},{6,7},{7,8},{8,9},{9,10},{10,1... | collective-permute-start | bytes 589832 | tf_op jit(solution)/shard_map/while/body/eval_jaxpr/ppermute | solution.py:25
  494.1 11.4 %collective-permute-start = (bf16[128,768]{1,0:T(8,128)(2,1)}, bf16[128,768]{1,0:T(8,128)(2,1)S(1)}, u32[]{:S(2)}, u32[]{:S(2)}) collective-permute-start(bf16[128,768]{1,0:T(8,128)(2,1)} %get-tuple-element.115), channel_id=1, source_target_pairs={{0,1},{1,2},{2,3},{3,4},{4,5},{5,6},{6,7},{7,8},{8,9},{9,10},{10,1... | collective-permute-start | bytes 589832 | tf_op jit(solution)/shard_map/while/body/eval_jaxpr/ppermute | solution.py:25
  506.8 11.4 %collective-permute-start = (bf16[128,768]{1,0:T(8,128)(2,1)}, bf16[128,768]{1,0:T(8,128)(2,1)S(1)}, u32[]{:S(2)}, u32[]{:S(2)}) collective-permute-start(bf16[128,768]{1,0:T(8,128)(2,1)} %get-tuple-element.115), channel_id=1, source_target_pairs={{0,1},{1,2},{2,3},{3,4},{4,5},{5,6},{6,7},{7,8},{8,9},{9,10},{10,1... | collective-permute-start | bytes 589832 | tf_op jit(solution)/shard_map/while/body/eval_jaxpr/ppermute | solution.py:25
  519.6 11.4 %collective-permute-start = (bf16[128,768]{1,0:T(8,128)(2,1)}, bf16[128,768]{1,0:T(8,128)(2,1)S(1)}, u32[]{:S(2)}, u32[]{:S(2)}) collective-permute-start(bf16[128,768]{1,0:T(8,128)(2,1)} %get-tuple-element.115), channel_id=1, source_target_pairs={{0,1},{1,2},{2,3},{3,4},{4,5},{5,6},{6,7},{7,8},{8,9},{9,10},{10,1... | collective-permute-start | bytes 589832 | tf_op jit(solution)/shard_map/while/body/eval_jaxpr/ppermute | solution.py:25
  532.4 11.4 %collective-permute-start = (bf16[128,768]{1,0:T(8,128)(2,1)}, bf16[128,768]{1,0:T(8,128)(2,1)S(1)}, u32[]{:S(2)}, u32[]{:S(2)}) collective-permute-start(bf16[128,768]{1,0:T(8,128)(2,1)} %get-tuple-element.115), channel_id=1, source_target_pairs={{0,1},{1,2},{2,3},{3,4},{4,5},{5,6},{6,7},{7,8},{8,9},{9,10},{10,1... | collective-permute-start | bytes 589832 | tf_op jit(solution)/shard_map/while/body/eval_jaxpr/ppermute | solution.py:25
  548.6 5.6 copy-start.11
  548.6 5.6 copy-start.14
  551.4 6.4 %copy-start.8 = (f32[128,32]{0,1:T(8,128)S(1)}, f32[128,32]{0,1:T(8,128)}, u32[]{:S(2)}) copy-start(f32[128,32]{0,1:T(8,128)} %get-tuple-element.80) | copy-start | bytes 49156
  551.4 6.4 %copy-start.9 = (f32[128,32]{0,1:T(8,128)S(1)}, f32[128,32]{0,1:T(8,128)}, u32[]{:S(2)}) copy-start(f32[128,32]{0,1:T(8,128)} %get-tuple-element.81) | copy-start | bytes 49156
  568.0 8.6 %copy-start.4 = (bf16[1664,384]{0,1:T(8,128)(2,1)S(1)}, bf16[1664,384]{0,1:T(8,128)(2,1)}, u32[]{:S(2)}) copy-start(bf16[1664,384]{0,1:T(8,128)(2,1)} %copy.58) | copy-start | bytes 3833860
  576.6 9.3 %copy-start.7 = (bf16[5,16,1152]{2,1,0:T(8,128)(2,1)S(1)}, bf16[5,16,1152]{2,1,0:T(8,128)(2,1)}, u32[]{:S(2)}) copy-start(bf16[5,16,1152]{2,1,0:T(8,128)(2,1)} %dot_general.51) | copy-start | bytes 552964
  576.6 9.3 %copy-start.16 = (f32[128,5]{0,1:T(8,128)S(1)}, f32[128,5]{0,1:T(8,128)}, u32[]{:S(2)}) copy-start(f32[128,5]{0,1:T(8,128)} %copy-done.15) | copy-start | bytes 7684
  576.6 9.5 %copy-start.5 = (bf16[80,1152]{1,0:T(8,128)(2,1)S(1)}, bf16[80,1152]{1,0:T(8,128)(2,1)}, u32[]{:S(2)}) copy-start(bf16[80,1152]{1,0:T(8,128)(2,1)} %reshape_reshape.9) | copy-start | bytes 552964
  576.6 9.7 %copy-start.2 = (bf16[1152,1152]{1,0:T(8,128)(2,1)S(1)}, bf16[1152,1152]{1,0:T(8,128)(2,1)}, u32[]{:S(2)}) copy-start(bf16[1152,1152]{1,0:T(8,128)(2,1)} %param.23) | copy-start | bytes 7962628
  (3 other events, 14.1 us)
Sparse Core Ops, SparseCore 0:
  10.8 65.1 all-gather.7
  79.5 62.7 all-gather.13
  145.3 62.7 all-gather.11
  210.9 62.7 all-gather.9
  277.0 65.9 all-gather.5
where the time goes:
time: 596 us; the launch traced here: 594 us
  waiting for transfers between devices  367 us (62%)
  local copies, waits for them, and re-layouts  138 us (23%)
  matrix products  29.9 us (5%)
  starting transfers between devices  23.3 us (4%)
  other arithmetic  21.5 us (4%)
  between operations  14.2 us (2%)
    ppermute x12, waiting for transfers between devices, from_behind(): return lax.ppermute(block, axis, route)  114 us
    reshape x6, local copies, waits for them, and re-layouts, on_device(): flat_all.reshape(tok_count, own_count * per_owner, table_shape[0], table_...  68.3 us
    all_gather x1, waiting for transfers between devices, on_device(): lax.all_gather(flat_o_in, ('tok', 'own'), axis=0, tiled=True)  53.3 us
    all_gather x1, waiting for transfers between devices, on_device(): lax.all_gather(flat_kv_out, ('tok', 'own'), axis=0, tiled=True)  53.1 us
    all_gather x1, waiting for transfers between devices, on_device(): lax.all_gather(flat_q_out, ('tok', 'own'), axis=0, tiled=True)  52.4 us
    all_gather x1, waiting for transfers between devices, on_device(): lax.all_gather(flat_qkv_in, ('tok', 'own'), axis=0, tiled=True)  48.8 us
    all_gather x1, waiting for transfers between devices, on_device(): lax.all_gather(flat_o_out, ('tok', 'own'), axis=0, tiled=True)  45.4 us
    ppermute x12, starting transfers between devices, from_behind(): return lax.ppermute(block, axis, route)  23.1 us
  transfers between devices with their start and end apart: 17, of which 17 were waited for; matrix products, arithmetic and copies ran while one was open for 14% of the time, Pallas kernels for 0%

commit v1 on v0

--- a/solution.py
+++ b/solution.py
@@ -120,33 +120,39 @@
     segment, offset, members = prompt_index(positions, lengths)
     prompt_count = lengths.shape[0]
     first_segment = segment[0]
-    segment_ids = jnp.minimum(
-        first_segment + jnp.arange(SEG_DEV, dtype=jnp.int32), prompt_count - 1
-    )
-    segment_hit = jnp.arange(prompt_count, dtype=jnp.int32)[None, :] == segment_ids[:, None]
-    needed_adapter = jnp.sum(jnp.where(segment_hit, prompt_adapter[None, :], 0), axis=1)
-    needed_slot = slot_lookup(needed_adapter, adapter_slot)
     code_rows = segment - first_segment
     normed = rms_norm(tokens, norm_gain)
-    table_shapes = tuple((table.shape[1:] for table in (qkv_in, q_out, kv_out, o_in, o_out)))
-    flat_qkv_in = qkv_in.reshape(per_owner, -1)
-    flat_q_out = q_out.reshape(per_owner, -1)
-    flat_kv_out = kv_out.reshape(per_owner, -1)
-    flat_o_in = o_in.reshape(per_owner, -1)
-    flat_o_out = o_out.reshape(per_owner, -1)
+    tables = (qkv_in, q_out, kv_out, o_in, o_out)
+    table_shapes = tuple((table.shape[1:] for table in tables))
+    packed = jnp.concatenate([table.reshape(per_owner, -1) for table in tables], axis=1)
+    all_slots = lax.all_gather(packed, "own", axis=0, tiled=True)
+    own_here = lax.axis_index("own")
+    group_blocks = jnp.arange(tok_count, dtype=jnp.int32) * own_count + own_here
+    prompt_starts = jnp.cumsum(lengths) - lengths
+    group_first = (
+        jnp.sum(
+            (group_blocks[:, None] * tok_rows >= prompt_starts[None, :]).astype(jnp.int32), axis=1
+        )
+        - 1
+    )
+    group_segments = jnp.minimum(
+        group_first[:, None] + jnp.arange(SEG_DEV, dtype=jnp.int32)[None, :], prompt_count - 1
+    )
+    group_slots = jnp.take(adapter_slot, jnp.take(prompt_adapter, group_segments))
+    outgoing = jnp.take(all_slots, group_slots.reshape(-1), axis=0).reshape(
+        tok_count, SEG_DEV, packed.shape[1]
+    )
+    incoming = lax.all_to_all(outgoing, "tok", 0, 0, tiled=True)
     selected = []
-    gathered = (
-        lax.all_gather(flat_qkv_in, ("tok", "own"), axis=0, tiled=True),
-        lax.all_gather(flat_q_out, ("tok", "own"), axis=0, tiled=True),
-        lax.all_gather(flat_kv_out, ("tok", "own"), axis=0, tiled=True),
-        lax.all_gather(flat_o_in, ("tok", "own"), axis=0, tiled=True),
-        lax.all_gather(flat_o_out, ("tok", "own"), axis=0, tiled=True),
-    )
-    for flat_all, table_shape in zip(gathered, table_shapes):
-        shaped = flat_all.reshape(tok_count, own_count * per_owner, table_shape[0], table_shape[1])
-        chosen = jnp.take(shaped, needed_slot, axis=1)
+    col = 0
+    for table_shape in table_shapes:
+        width = table_shape[0] * table_shape[1]
+        piece = incoming[:, :, col : col + width].reshape(
+            tok_count, SEG_DEV, table_shape[0], table_shape[1]
+        )
+        col += width
         selected.append(
-            jnp.transpose(chosen, (1, 2, 0, 3)).reshape(
+            jnp.transpose(piece, (1, 2, 0, 3)).reshape(
                 SEG_DEV, table_shape[0], tok_count * table_shape[1]
             )
         )
@@ -169,15 +175,13 @@
     key_store = jnp.zeros(((REACH + 1) * tok_rows, 2 * KVW), jnp.bfloat16)
     key_store = lax.dynamic_update_slice_in_dim(key_store, key_value, REACH * tok_rows, 0)
 
-    def advance(turn_index, loop_carry):
-        moving, stored = loop_carry
+    window = key_store
+    moving = key_value
+    for turn_index in range(REACH):
         moving = from_behind(moving, ("tok", "own"), 1)
-        stored = lax.dynamic_update_slice_in_dim(
-            stored, moving, (REACH - 1 - turn_index) * tok_rows, 0
-        )
-        return (moving, stored)
-
-    window = lax.fori_loop(0, REACH, advance, (key_value, key_store))[1]
+        window = lax.dynamic_update_slice_in_dim(
+            window, moving, (REACH - 1 - turn_index) * tok_rows, 0
+        )
     key_positions = (
         device_here * tok_rows
         - REACH * tok_rows

time: 596 us -> 276 us (0.46)
  waiting for transfers between devices: 367 us -> 118 us
  local copies, waits for them, and re-layouts: 138 us -> 62.1 us
  blocking collectives: 0 us -> 15 us
  between operations: 14.2 us -> 1.59 us
  starting transfers between devices: 23.3 us -> 31.7 us
    all_gather x5 -> x0, waiting for transfers between devices: 253 us -> none  [the longest x1 53.3 us: on_device(): lax.all_gather(flat_o_in, ('tok', 'own'), axis=0, tiled=True)]
    reshape x11 -> x12, local copies, waits for them, and re-layouts: 75.1 us -> 14.5 us  [the longest x5 9 us: on_device(): incoming[:, :, col:col + width]]
    all_to_all x0 -> x1, waiting for transfers between devices: none -> 25 us  [on_device(): incoming = lax.all_to_all(outgoing, 'tok', 0, 0, tiled=True)]
    ppermute x12, waiting for transfers between devices: 114 us -> 92.7 us  [from_behind(): return lax.ppermute(block, axis, route)]
    all_gather x0 -> x1, blocking collectives: none -> 15 us  [on_device(): all_slots = lax.all_gather(packed, 'own', axis=0, tiled=True)]
    gather x5 -> x6, local copies, waits for them, and re-layouts: 19.7 us -> 10.1 us  [the longest x2 7.45 us: on_device(): jnp.take(all_slots, group_slots.reshape(-1), axis=0)]
    all_to_all x0 -> x1, starting transfers between devices: none -> 8.54 us  [on_device(): incoming = lax.all_to_all(outgoing, 'tok', 0, 0, tiled=True)]
    slice x0 -> x8, local copies, waits for them, and re-layouts: none -> 8.28 us  [on_device(): incoming[:, :, col:col + width]]
  transfers between devices with their start and end apart: 17 -> 13, of which waited for: 17 -> 12; matrix products, arithmetic and copies ran while one was open for 14% -> 11% of each run, Pallas kernels for 0% -> 0%
where the time goes in v1:
time: 276 us; the launch traced here: 274 us
  waiting for transfers between devices  118 us (43%)
  local copies, waits for them, and re-layouts  62.1 us (22%)
  starting transfers between devices  31.7 us (11%)
  matrix products  28.8 us (10%)
  other arithmetic  16.9 us (6%)
  blocking collectives  15 us (5%)
    ppermute x12, waiting for transfers between devices, from_behind(): return lax.ppermute(block, axis, route)  92.7 us
    all_to_all x1, waiting for transfers between devices, on_device(): incoming = lax.all_to_all(outgoing, 'tok', 0, 0, tiled=True)  25 us
    ppermute x12, starting transfers between devices, from_behind(): return lax.ppermute(block, axis, route)  23.1 us
    all_gather x1, blocking collectives, on_device(): all_slots = lax.all_gather(packed, 'own', axis=0, tiled=True)  15 us
    dot_general x1, matrix products, on_device(): jnp.einsum('iyxv,vip->xiyp', rounded_values, value_head_rows, preferred_e...  9.21 us
    reshape x5, local copies, waits for them, and re-layouts, on_device(): incoming[:, :, col:col + width]  9 us
    dot_general x1, matrix products, on_device(): jnp.einsum('qkzr,ckr->kzqc', query_head_rows, key_head_rows, preferred_el...  8.99 us
    reduce_sum x1, other arithmetic, on_device(): row_total = jnp.sum(exp_scores, axis=-1)  8.61 us
  transfers between devices with their start and end apart: 13, of which 12 were waited for; matrix products, arithmetic and copies ran while one was open for 11% of the time, Pallas kernels for 0%

profile of v1, /device:TPU:8, one launch (start us, length us, event | category | flops | bytes accessed | tf_op | source)
XLA Modules:
  0.0 273.7 jit_solution(17576496565474559692)
XLA Ops:
  9.0 15.0 %all_gather.3 = bf16[64,7680]{1,0:T(8,128)(2,1)} all-gather(bf16[8,7680]{1,0:T(8,128)(2,1)S(1)} %constant_dynamic-update-slice_fusion), channel_id=1, replica_groups=mesh['tok'=16,'own'=8] {'own'}, dimensions={0}, use_global_device_ids=true | all-gather | bytes 1105920 | tf_op jit(solution)/shard_map/all_gather | solution.py:128
  24.0 4.8 %gather_fusion = bf16[80,7680]{1,0:T(8,128)(2,1)} fusion(bf16[64,7680]{1,0:T(8,128)(2,1)} %all_gather.3, s32[1024]{0:T(1024)S(1)} %pad_clamp_fusion), kind=kCustom, calls=%fused_computation.2 | custom fusion | bytes 2457920 | tf_op jit(solution)/shard_map/jit(_take)/gather | solution.py:142
  28.8 2.6 gather.10
  31.5 3.1 %broadcast_select_fusion = bf16[16,5,7680]{2,1,0:T(8,128)(2,1)} fusion(bf16[16,5,7680]{2,1,0:T(8,128)(2,1)} %gather.10, pred[16,5]{1,0:T(8,128)(4,1)S(1)} %get-tuple-element.3), kind=kLoop, calls=%fused_computation.18 | loop fusion | flops 614400 | bytes 2457680 | tf_op jit(solution)/shard_map/jit(_take)/select_n | solution.py:142
  34.6 8.5 %all-to-all-start = ((bf16[16,5,7680]{2,1,0:T(8,128)(2,1)}), bf16[16,5,7680]{2,1,0:T(8,128)(2,1)}, u32[]{:S(2)}, u32[]{:S(2)}) async-start(bf16[16,5,7680]{2,1,0:T(8,128)(2,1)} %broadcast_select_fusion), calls=%async_computation | async-start | bytes 3932160 | tf_op jit(solution)/shard_map/all_to_all | solution.py:145
  45.1 25.0 %all-to-all-done = bf16[16,5,7680]{2,1,0:T(8,128)(2,1)} async-done(((bf16[16,5,7680]{2,1,0:T(8,128)(2,1)}), bf16[16,5,7680]{2,1,0:T(8,128)(2,1)}, u32[]{:S(2)}, u32[]{:S(2)}) %all-to-all-start) | async-done | bytes 1228832 | tf_op jit(solution)/shard_map/all_to_all | solution.py:145
  73.0 2.2 copy.47
  75.1 2.3 reshape.335
  78.8 2.7 reshape.333
  81.5 2.4 copy.45
  83.9 2.2 dot_general.41
  94.9 9.3 %collective-permute-done = bf16[128,768]{1,0:T(8,128)(2,1)S(1)} collective-permute-done((bf16[128,768]{1,0:T(8,128)(2,1)S(1)}, bf16[128,768]{1,0:T(8,128)(2,1)S(1)}, u32[]{:S(2)}, u32[]{:S(2)}) %collective-permute-start) | collective-permute-done | bytes 196640 | tf_op jit(solution)/shard_map/ppermute | solution.py:25
  104.2 2.1 collective-permute-start.1
  107.3 8.1 %collective-permute-done.1 = bf16[128,768]{1,0:T(8,128)(2,1)} collective-permute-done((bf16[128,768]{1,0:T(8,128)(2,1)S(1)}, bf16[128,768]{1,0:T(8,128)(2,1)}, u32[]{:S(2)}, u32[]{:S(2)}) %collective-permute-start.1) | collective-permute-done | bytes 196640 | tf_op jit(solution)/shard_map/ppermute | solution.py:25
  117.4 2.0 fusion.43
  123.7 2.0 reshape_reshape.9
  139.8 8.5 %collective-permute-done.3 = bf16[128,768]{1,0:T(8,128)(2,1)S(1)} collective-permute-done((bf16[128,768]{1,0:T(8,128)(2,1)}, bf16[128,768]{1,0:T(8,128)(2,1)S(1)}, u32[]{:S(2)}, u32[]{:S(2)}) %collective-permute-start.3) | collective-permute-done | bytes 196640 | tf_op jit(solution)/shard_map/ppermute | solution.py:25
  150.3 2.2 convolution_add_fusion.1
  152.4 2.1 copy.54
  154.8 4.8 %collective-permute-done.4 = bf16[128,768]{1,0:T(8,128)(2,1)} collective-permute-done((bf16[128,768]{1,0:T(8,128)(2,1)S(1)}, bf16[128,768]{1,0:T(8,128)(2,1)}, u32[]{:S(2)}, u32[]{:S(2)}) %collective-permute-start.4) | collective-permute-done | bytes 196640 | tf_op jit(solution)/shard_map/ppermute | solution.py:25
  161.7 9.4 %collective-permute-done.5 = bf16[128,768]{1,0:T(8,128)(2,1)S(1)} collective-permute-done((bf16[128,768]{1,0:T(8,128)(2,1)}, bf16[128,768]{1,0:T(8,128)(2,1)S(1)}, u32[]{:S(2)}, u32[]{:S(2)}) %collective-permute-start.5) | collective-permute-done | bytes 196640 | tf_op jit(solution)/shard_map/ppermute | solution.py:25
  173.0 9.2 %collective-permute-done.6 = bf16[128,768]{1,0:T(8,128)(2,1)S(1)} collective-permute-done((bf16[128,768]{1,0:T(8,128)(2,1)S(1)}, bf16[128,768]{1,0:T(8,128)(2,1)S(1)}, u32[]{:S(2)}, u32[]{:S(2)}) %collective-permute-start.6) | collective-permute-done | bytes 196640 | tf_op jit(solution)/shard_map/ppermute | solution.py:25
  186.0 7.4 %collective-permute-done.7 = bf16[128,768]{1,0:T(8,128)(2,1)S(1)} collective-permute-done((bf16[128,768]{1,0:T(8,128)(2,1)S(1)}, bf16[128,768]{1,0:T(8,128)(2,1)S(1)}, u32[]{:S(2)}, u32[]{:S(2)}) %collective-permute-start.7) | collective-permute-done | bytes 196640 | tf_op jit(solution)/shard_map/ppermute | solution.py:25
  196.3 8.3 %collective-permute-done.8 = bf16[128,768]{1,0:T(8,128)(2,1)S(1)} collective-permute-done((bf16[128,768]{1,0:T(8,128)(2,1)S(1)}, bf16[128,768]{1,0:T(8,128)(2,1)S(1)}, u32[]{:S(2)}, u32[]{:S(2)}) %collective-permute-start.8) | collective-permute-done | bytes 196640 | tf_op jit(solution)/shard_map/ppermute | solution.py:25
  206.6 9.2 %collective-permute-done.9 = bf16[128,768]{1,0:T(8,128)(2,1)S(1)} collective-permute-done((bf16[128,768]{1,0:T(8,128)(2,1)S(1)}, bf16[128,768]{1,0:T(8,128)(2,1)S(1)}, u32[]{:S(2)}, u32[]{:S(2)}) %collective-permute-start.9) | collective-permute-done | bytes 196640 | tf_op jit(solution)/shard_map/ppermute | solution.py:25
  217.8 9.2 %collective-permute-done.10 = bf16[128,768]{1,0:T(8,128)(2,1)S(1)} collective-permute-done((bf16[128,768]{1,0:T(8,128)(2,1)S(1)}, bf16[128,768]{1,0:T(8,128)(2,1)S(1)}, u32[]{:S(2)}, u32[]{:S(2)}) %collective-permute-start.10) | collective-permute-done | bytes 196640 | tf_op jit(solution)/shard_map/ppermute | solution.py:25
  229.0 9.2 %collective-permute-done.11 = bf16[128,768]{1,0:T(8,128)(2,1)S(1)} collective-permute-done((bf16[128,768]{1,0:T(8,128)(2,1)S(1)}, bf16[128,768]{1,0:T(8,128)(2,1)S(1)}, u32[]{:S(2)}, u32[]{:S(2)}) %collective-permute-start.11) | collective-permute-done | bytes 196640 | tf_op jit(solution)/shard_map/ppermute | solution.py:25
  240.0 2.5 copy.51
  242.5 2.5 copy.50
  245.0 9.0 %fusion.2 = (f32[6,3,128]{2,1,0:T(4,128)S(1)}, f32[6,1664,128,3]{2,1,3,0:T(8,128)}) fusion(pred[128,1664]{0,1:T(8,128)(4,1)S(1)} %compare_and_fusion, bf16[1664,6,64,1]{0,2,3,1:T(8,128)(2,1)} %bitcast.101, bf16[128,6,3,64]{0,3,2,1:T(8,128)(2,1)S(1)} %bitcast.105), kind=kOutput, calls=%fused_computation.7 | convolution fusion | flops 502232832 | bytes 17130496 | tf_op jit(solution)/shard_map/qkzr,ckr->kzqc/dot_general | solution.py:199
  254.0 8.6 %fusion = f32[6,3,128]{2,1,0:T(4,128)S(1)} fusion(f32[6,1664,128,3]{2,1,3,0:T(8,128)} %get-tuple-element.17, f32[6,3,128]{2,1,0:T(4,128)S(1)} %get-tuple-element.16, pred[128,1664]{0,1:T(8,128)(4,1)S(1)} %compare_and_fusion), kind=kLoop, calls=%fused_computation.5 | loop fusion | flops 15333120 | bytes 15566848 | tf_op jit(solution)/shard_map/reduce_sum | solution.py:205
  262.6 9.2 %fusion.23 = bf16[128,6,3,64]{0,3,2,1:T(8,128)(2,1)S(1)} fusion(bf16[1664,6,64,1]{0,2,3,1:T(8,128)(2,1)S(1)} %bitcast.109, f32[6,1664,128,3]{2,1,3,0:T(8,128)} %get-tuple-element.17, f32[6,3,128]{2,1,0:T(4,128)S(1)} %get-tuple-element.16, pred[128,1664]{0,1:T(8,128)(4,1)S(1)} %compare_and_fusion, f32[128,6,3]{0,2,1:T(4,128)S(1)} %bitcast.116), kind=kOutput, calls=%fused_computation.34 | convolution fusion | flops 506363904 | bytes 17139712 | tf_op jit(solution)/shard_map/iyxv,vip->xiyp/dot_general | solution.py:207
  (173 shorter events, 66.3 us)
Async XLA Ops:
  0.6 149.6 %copy-start = (bf16[1152,1152]{1,0:T(8,128)(2,1)S(1)}, bf16[1152,1152]{1,0:T(8,128)(2,1)}, u32[]{:S(2)}) copy-start(bf16[1152,1152]{1,0:T(8,128)(2,1)} %param.18) | copy-start | bytes 7962628
  34.6 9.7 %copy-start.26 = (bf16[1152]{0:T(1024)(128)(2,1)S(1)}, bf16[1152]{0:T(1024)(128)(2,1)}, u32[]{:S(2)}) copy-start(bf16[1152]{0:T(1024)(128)(2,1)} %param.17) | copy-start | bytes 6916
  34.6 35.5 %all-to-all-start = ((bf16[16,5,7680]{2,1,0:T(8,128)(2,1)}), bf16[16,5,7680]{2,1,0:T(8,128)(2,1)}, u32[]{:S(2)}, u32[]{:S(2)}) async-start(bf16[16,5,7680]{2,1,0:T(8,128)(2,1)} %broadcast_select_fusion), calls=%async_computation | async-start | bytes 3932160 | tf_op jit(solution)/shard_map/all_to_all | solution.py:145
  43.1 27.0 %copy-start.29 = (s32[128]{0:T(128)}, s32[128]{0:T(128)S(1)}, u32[]{:S(2)}) copy-start(s32[128]{0:T(128)S(1)} %iota_add_fusion.1) | copy-start | bytes 1540
  43.4 26.7 %copy-start.31 = (s32[128]{0:T(128)}, s32[128]{0:T(128)S(1)}, u32[]{:S(2)}) copy-start(s32[128]{0:T(128)S(1)} %broadcast_add_fusion.1) | copy-start | bytes 1540
  44.3 41.8 %copy-start.18 = (f32[1152]{0:T(1024)}, f32[1152]{0:T(1024)S(1)}, u32[]{:S(2)}) copy-start(f32[1152]{0:T(1024)S(1)} %convert_element_type.91) | copy-start | bytes 13828
  44.3 41.8 %copy-start.25 = (f32[128]{0:T(128)}, f32[128]{0:T(128)S(1)}, u32[]{:S(2)}) copy-start(f32[128]{0:T(128)S(1)} %add_rsqrt_fusion) | copy-start | bytes 1540
  44.4 41.7 %copy-start.27 = (f32[128,5]{0,1:T(8,128)}, f32[128,5]{0,1:T(8,128)S(1)}, u32[]{:S(2)}) copy-start(f32[128,5]{0,1:T(8,128)S(1)} %fusion.34) | copy-start | bytes 7684
  45.1 45.3 %copy-start.15 = (f32[128,32]{0,1:T(8,128)}, f32[128,32]{0,1:T(8,128)S(1)}, u32[]{:S(2)}) copy-start(f32[128,32]{0,1:T(8,128)S(1)} %get-tuple-element.14) | copy-start | bytes 49156
  90.4 15.9 %copy-start.21 = (s32[1664]{0:T(1024)S(1)}, s32[1664]{0:T(1024)}, u32[]{:S(2)}) copy-start(s32[1664]{0:T(1024)} %copy-done.20) | copy-start | bytes 19972
  90.4 15.9 %copy-start.30 = (s32[128]{0:T(128)S(1)}, s32[128]{0:T(128)}, u32[]{:S(2)}) copy-start(s32[128]{0:T(128)} %copy-done.29) | copy-start | bytes 1540
  90.4 15.9 %copy-start.32 = (s32[128]{0:T(128)S(1)}, s32[128]{0:T(128)}, u32[]{:S(2)}) copy-start(s32[128]{0:T(128)} %copy-done.31) | copy-start | bytes 1540
  92.9 22.5 %copy-start.7 = (bf16[128,768]{1,0:T(8,128)(2,1)}, bf16[128,768]{1,0:T(8,128)(2,1)S(1)}, u32[]{:S(2)}) copy-start(bf16[128,768]{1,0:T(8,128)(2,1)S(1)} %pad_maximum_fusion.1) | copy-start | bytes 589828
  92.9 11.2 %collective-permute-start = (bf16[128,768]{1,0:T(8,128)(2,1)S(1)}, bf16[128,768]{1,0:T(8,128)(2,1)S(1)}, u32[]{:S(2)}, u32[]{:S(2)}) collective-permute-start(bf16[128,768]{1,0:T(8,128)(2,1)S(1)} %pad_maximum_fusion.1), channel_id=1, source_target_pairs={{0,1},{1,2},{2,3},{3,4},{4,5},{5,6},{6,7},{7,8},{8,9},{9,10},{10,1... | collective-permute-start | bytes 589832 | tf_op jit(solution)/shard_map/ppermute | solution.py:25
  104.2 11.3 %copy-start.10 = (bf16[128,768]{1,0:T(8,128)(2,1)}, bf16[128,768]{1,0:T(8,128)(2,1)S(1)}, u32[]{:S(2)}) copy-start(bf16[128,768]{1,0:T(8,128)(2,1)S(1)} %collective-permute-done) | copy-start | bytes 589828
  104.2 11.3 %collective-permute-start.1 = (bf16[128,768]{1,0:T(8,128)(2,1)S(1)}, bf16[128,768]{1,0:T(8,128)(2,1)}, u32[]{:S(2)}, u32[]{:S(2)}) collective-permute-start(bf16[128,768]{1,0:T(8,128)(2,1)S(1)} %collective-permute-done), channel_id=1, source_target_pairs={{0,1},{1,2},{2,3},{3,4},{4,5},{5,6},{6,7},{7,8},{8,9},{9,10},{10,1... | collective-permute-start | bytes 589832 | tf_op jit(solution)/shard_map/ppermute | solution.py:25
  115.5 21.4 %collective-permute-start.2 = (bf16[128,768]{1,0:T(8,128)(2,1)}, bf16[128,768]{1,0:T(8,128)(2,1)}, u32[]{:S(2)}, u32[]{:S(2)}) collective-permute-start(bf16[128,768]{1,0:T(8,128)(2,1)} %collective-permute-done.1), channel_id=1, source_target_pairs={{0,1},{1,2},{2,3},{3,4},{4,5},{5,6},{6,7},{7,8},{8,9},{9,10},{10,1... | collective-permute-start | bytes 589832 | tf_op jit(solution)/shard_map/ppermute | solution.py:25
  136.9 11.4 %collective-permute-start.3 = (bf16[128,768]{1,0:T(8,128)(2,1)}, bf16[128,768]{1,0:T(8,128)(2,1)S(1)}, u32[]{:S(2)}, u32[]{:S(2)}) collective-permute-start(bf16[128,768]{1,0:T(8,128)(2,1)} %collective-permute-done.2), channel_id=1, source_target_pairs={{0,1},{1,2},{2,3},{3,4},{4,5},{5,6},{6,7},{7,8},{8,9},{9,10},{10,1... | collective-permute-start | bytes 589832 | tf_op jit(solution)/shard_map/ppermute | solution.py:25
  139.8 14.8 %copy-start.8 = (bf16[128,768]{1,0:T(8,128)(2,1)S(1)}, bf16[128,768]{1,0:T(8,128)(2,1)}, u32[]{:S(2)}) copy-start(bf16[128,768]{1,0:T(8,128)(2,1)} %copy-done.7) | copy-start | bytes 589828
  148.3 11.3 %collective-permute-start.4 = (bf16[128,768]{1,0:T(8,128)(2,1)S(1)}, bf16[128,768]{1,0:T(8,128)(2,1)}, u32[]{:S(2)}, u32[]{:S(2)}) collective-permute-start(bf16[128,768]{1,0:T(8,128)(2,1)S(1)} %collective-permute-done.3), channel_id=1, source_target_pairs={{0,1},{1,2},{2,3},{3,4},{4,5},{5,6},{6,7},{7,8},{8,9},{9,10},{10,1... | collective-permute-start | bytes 589832 | tf_op jit(solution)/shard_map/ppermute | solution.py:25
  154.6 18.4 %copy-start.11 = (bf16[128,768]{1,0:T(8,128)(2,1)S(1)}, bf16[128,768]{1,0:T(8,128)(2,1)}, u32[]{:S(2)}) copy-start(bf16[128,768]{1,0:T(8,128)(2,1)} %copy-done.10) | copy-start | bytes 589828
  154.8 40.6 %copy-start.13 = (bf16[128,768]{1,0:T(8,128)(2,1)S(1)}, bf16[128,768]{1,0:T(8,128)(2,1)}, u32[]{:S(2)}) copy-start(bf16[128,768]{1,0:T(8,128)(2,1)} %copy-done.12) | copy-start | bytes 589828
  159.6 11.4 %collective-permute-start.5 = (bf16[128,768]{1,0:T(8,128)(2,1)}, bf16[128,768]{1,0:T(8,128)(2,1)S(1)}, u32[]{:S(2)}, u32[]{:S(2)}) collective-permute-start(bf16[128,768]{1,0:T(8,128)(2,1)} %collective-permute-done.4), channel_id=1, source_target_pairs={{0,1},{1,2},{2,3},{3,4},{4,5},{5,6},{6,7},{7,8},{8,9},{9,10},{10,1... | collective-permute-start | bytes 589832 | tf_op jit(solution)/shard_map/ppermute | solution.py:25
  171.0 11.2 %collective-permute-start.6 = (bf16[128,768]{1,0:T(8,128)(2,1)S(1)}, bf16[128,768]{1,0:T(8,128)(2,1)S(1)}, u32[]{:S(2)}, u32[]{:S(2)}) collective-permute-start(bf16[128,768]{1,0:T(8,128)(2,1)S(1)} %collective-permute-done.5), channel_id=1, source_target_pairs={{0,1},{1,2},{2,3},{3,4},{4,5},{5,6},{6,7},{7,8},{8,9},{9,10},{10,1... | collective-permute-start | bytes 589832 | tf_op jit(solution)/shard_map/ppermute | solution.py:25
  182.2 11.2 %collective-permute-start.7 = (bf16[128,768]{1,0:T(8,128)(2,1)S(1)}, bf16[128,768]{1,0:T(8,128)(2,1)S(1)}, u32[]{:S(2)}, u32[]{:S(2)}) collective-permute-start(bf16[128,768]{1,0:T(8,128)(2,1)S(1)} %collective-permute-done.6), channel_id=1, source_target_pairs={{0,1},{1,2},{2,3},{3,4},{4,5},{5,6},{6,7},{7,8},{8,9},{9,10},{10,1... | collective-permute-start | bytes 589832 | tf_op jit(solution)/shard_map/ppermute | solution.py:25
  193.4 11.2 %collective-permute-start.8 = (bf16[128,768]{1,0:T(8,128)(2,1)S(1)}, bf16[128,768]{1,0:T(8,128)(2,1)S(1)}, u32[]{:S(2)}, u32[]{:S(2)}) collective-permute-start(bf16[128,768]{1,0:T(8,128)(2,1)S(1)} %collective-permute-done.7), channel_id=1, source_target_pairs={{0,1},{1,2},{2,3},{3,4},{4,5},{5,6},{6,7},{7,8},{8,9},{9,10},{10,1... | collective-permute-start | bytes 589832 | tf_op jit(solution)/shard_map/ppermute | solution.py:25
  204.6 11.2 %collective-permute-start.9 = (bf16[128,768]{1,0:T(8,128)(2,1)S(1)}, bf16[128,768]{1,0:T(8,128)(2,1)S(1)}, u32[]{:S(2)}, u32[]{:S(2)}) collective-permute-start(bf16[128,768]{1,0:T(8,128)(2,1)S(1)} %collective-permute-done.8), channel_id=1, source_target_pairs={{0,1},{1,2},{2,3},{3,4},{4,5},{5,6},{6,7},{7,8},{8,9},{9,10},{10,1... | collective-permute-start | bytes 589832 | tf_op jit(solution)/shard_map/ppermute | solution.py:25
  215.8 11.2 %collective-permute-start.10 = (bf16[128,768]{1,0:T(8,128)(2,1)S(1)}, bf16[128,768]{1,0:T(8,128)(2,1)S(1)}, u32[]{:S(2)}, u32[]{:S(2)}) collective-permute-start(bf16[128,768]{1,0:T(8,128)(2,1)S(1)} %collective-permute-done.9), channel_id=1, source_target_pairs={{0,1},{1,2},{2,3},{3,4},{4,5},{5,6},{6,7},{7,8},{8,9},{9,10},{10,1... | collective-permute-start | bytes 589832 | tf_op jit(solution)/shard_map/ppermute | solution.py:25
  227.0 11.2 %collective-permute-start.11 = (bf16[128,768]{1,0:T(8,128)(2,1)S(1)}, bf16[128,768]{1,0:T(8,128)(2,1)S(1)}, u32[]{:S(2)}, u32[]{:S(2)}) collective-permute-start(bf16[128,768]{1,0:T(8,128)(2,1)S(1)} %collective-permute-done.10), channel_id=1, source_target_pairs={{0,1},{1,2},{2,3},{3,4},{4,5},{5,6},{6,7},{7,8},{8,9},{9,10},{10,1... | collective-permute-start | bytes 589832 | tf_op jit(solution)/shard_map/ppermute | solution.py:25
  262.6 9.3 %copy-start.14 = (bf16[5,16,1152]{2,1,0:T(8,128)(2,1)S(1)}, bf16[5,16,1152]{2,1,0:T(8,128)(2,1)}, u32[]{:S(2)}) copy-start(bf16[5,16,1152]{2,1,0:T(8,128)(2,1)} %dot_general.51) | copy-start | bytes 552964
  262.6 9.5 %copy-start.9 = (bf16[80,1152]{1,0:T(8,128)(2,1)S(1)}, bf16[80,1152]{1,0:T(8,128)(2,1)}, u32[]{:S(2)}) copy-start(bf16[80,1152]{1,0:T(8,128)(2,1)} %reshape_reshape.9) | copy-start | bytes 552964
  262.6 9.7 %copy-start.4 = (bf16[1152,1152]{1,0:T(8,128)(2,1)S(1)}, bf16[1152,1152]{1,0:T(8,128)(2,1)}, u32[]{:S(2)}) copy-start(bf16[1152,1152]{1,0:T(8,128)(2,1)} %param.21) | copy-start | bytes 7962628
  (14 other events, 70.9 us)
